TPU v7x, 256 devices: a whole 4x4x8 slice. The times are simulated.
256 devices in a mesh: seq: 32 (over z_lo, y, core), head: 8 (over x, z_hi).
Axes of the slice: x: 4, y: 4, z: 8 (z_hi: 2, z_lo: 4; z = z_hi * 4 + z_lo), core: 2. Of those that a mesh axis runs over, the one named last changes fastest.
Arguments:
- queries: bfloat16 [16384, 1024], P('seq', 'head'), may hold values from -2.5 to 2.5
- keys: bfloat16 [16384, 1024], P('seq', 'head'), may hold values from -2.5 to 2.5
- values: bfloat16 [16384, 1024], P('seq', 'head'), may hold values from -6 to 6
- attn_out: bfloat16 [16384, 1024], P('seq', 'head'), may hold values from -6 to 6
- out_grad: bfloat16 [16384, 1024], P('seq', 'head'), may hold values from -6 to 6
- lse: float32 [8, 16384], P('head', 'seq'), may hold values from 3.5 to 5.5
- trace_id: int32 [16384], replicated, may hold values from 0 to 127, never falling along the last dimension, each value on 1 to 384 neighbouring positions
- key_tiles: int32 [128, 48], P('seq'), may hold values from 0 to 127, as said below
- tile_count: int32 [128], P('seq'), may hold values from 1 to 48, as said below
- w_query: bfloat16 [1024, 1024], P(None, 'head'), may hold values from -0.1875 to 0.1875
- w_key: bfloat16 [1024, 1024], P(None, 'head'), may hold values from -0.1875 to 0.1875
- w_value: bfloat16 [1024, 1024], P(None, 'head'), may hold values from -0.1875 to 0.1875
- w_out: bfloat16 [1024, 1024], P('head'), may hold values from -0.1875 to 0.1875
Outputs:
- d_input: bfloat16 [16384, 1024], P('seq', 'head')
Inputs may be any that keep to these rules, and one draw needn't show every extreme that they name: `key_tiles`: each row lists 48 different key tiles and never its own tile; entries from position tile_count onward are not used. `tile_count`: some query tile uses all 48 entries. `trace_id`: trace numbers never fall along the tokens; one trace spans 384 tokens, none more.
All inputs are finite; a program needn't handle non-finite values.
Results may differ from a plain program's by a relative error of at most 0.015.
Values may be sent and summed in bfloat16 or wider, within the bound.
No kernel may reach another device: no remote copies, remote signals or barrier semaphores. Data moves between devices by JAX's collectives and lax.ppermute only.
A program may use at most 64 MiB of HBM per device.

v0:
```python
import jax
import jax.numpy as jnp
from jax import lax
from jax.sharding import PartitionSpec as P

HD = 128
TILE = 128
SEL = 48


def from_behind(value, axis, by):
    count = lax.axis_size(axis)
    return lax.ppermute(value, axis, [(i, (i + by) % count) for i in range(count)])


def pair_grads(query_heads, key_heads, value_heads, grad_heads, norm_rows, delta_rows, admit):
    scale = query_heads.shape[-1] ** (-0.5)
    scores = (
        jnp.einsum("rhd,chd->hrc", query_heads, key_heads, preferred_element_type=jnp.float32)
        * scale
    )
    probs = jnp.where(admit[None], jnp.exp(scores - norm_rows[:, :, None]), 0.0)
    value_grad = jnp.einsum(
        "hrc,rhd->chd", probs.astype(jnp.bfloat16), grad_heads, preferred_element_type=jnp.float32
    )
    prob_grad = jnp.einsum(
        "rhd,chd->hrc", grad_heads, value_heads, preferred_element_type=jnp.float32
    )
    score_grad = (probs * (prob_grad - delta_rows[:, :, None]) * scale).astype(jnp.bfloat16)
    query_grad = jnp.einsum(
        "hrc,chd->rhd", score_grad, key_heads, preferred_element_type=jnp.float32
    )
    key_grad = jnp.einsum(
        "hrc,rhd->chd", score_grad, query_heads, preferred_element_type=jnp.float32
    )
    return (query_grad, key_grad, value_grad)


def query_grads(query_heads, key_heads, value_heads, grad_heads, norm_rows, delta_rows, admit):
    scale = query_heads.shape[-1] ** (-0.5)
    scores = (
        jnp.einsum("rhd,chd->hrc", query_heads, key_heads, preferred_element_type=jnp.float32)
        * scale
    )
    probs = jnp.where(admit[None], jnp.exp(scores - norm_rows[:, :, None]), 0.0)
    prob_grad = jnp.einsum(
        "rhd,chd->hrc", grad_heads, value_heads, preferred_element_type=jnp.float32
    )
    score_grad = (probs * (prob_grad - delta_rows[:, :, None]) * scale).astype(jnp.bfloat16)
    return jnp.einsum("hrc,chd->rhd", score_grad, key_heads, preferred_element_type=jnp.float32)


def key_grads(query_heads, key_heads, value_heads, grad_heads, norm_rows, delta_rows, admit):
    scale = query_heads.shape[-1] ** (-0.5)
    scores = (
        jnp.einsum("rhd,chd->hrc", query_heads, key_heads, preferred_element_type=jnp.float32)
        * scale
    )
    probs = jnp.where(admit[None], jnp.exp(scores - norm_rows[:, :, None]), 0.0)
    value_grad = jnp.einsum(
        "hrc,rhd->chd", probs.astype(jnp.bfloat16), grad_heads, preferred_element_type=jnp.float32
    )
    prob_grad = jnp.einsum(
        "rhd,chd->hrc", grad_heads, value_heads, preferred_element_type=jnp.float32
    )
    score_grad = (probs * (prob_grad - delta_rows[:, :, None]) * scale).astype(jnp.bfloat16)
    key_grad = jnp.einsum(
        "hrc,rhd->chd", score_grad, query_heads, preferred_element_type=jnp.float32
    )
    return (key_grad, value_grad)


def settle(total):
    part = lax.optimization_barrier(total.astype(jnp.bfloat16))
    return part.astype(jnp.float32)


def per_device(
    queries,
    keys,
    values,
    attn_out,
    out_grad,
    lse,
    trace_id,
    key_tiles,
    tile_count,
    w_query,
    w_key,
    w_value,
    w_out,
):
    tokens_here, width = queries.shape
    heads_here = width // HD
    seq_count = lax.axis_size("seq")
    seq_index = lax.axis_index("seq")
    tiles_here = tokens_here // TILE
    head_count = lax.axis_size("head")
    head_index = lax.axis_index("head")
    grad_blocks = [out_grad] + [from_behind(out_grad, "head", shift) for shift in range(1, head_count)]
    block_order = (head_index - jnp.arange(head_count)) % head_count
    block_width = out_grad.shape[1]
    w_out_blocks = jnp.take(
        w_out.reshape(w_out.shape[0], head_count, block_width), block_order, axis=1
    ).reshape(w_out.shape[0], head_count * block_width)
    d_attn = lax.dot_general(
        jnp.concatenate(grad_blocks, axis=1),
        w_out_blocks,
        (((1,), (1,)), ((), ())),
        preferred_element_type=jnp.float32,
    ).astype(jnp.bfloat16)
    product = d_attn.astype(jnp.float32) * attn_out.astype(jnp.float32)
    delta = jnp.sum(product.reshape(tokens_here, heads_here, HD), axis=2).T
    query_heads = queries.reshape(tokens_here, heads_here, HD)
    key_heads = keys.reshape(tokens_here, heads_here, HD)
    value_heads = values.reshape(tokens_here, heads_here, HD)
    grad_heads = d_attn.reshape(tokens_here, heads_here, HD)
    trace_here = lax.dynamic_slice_in_dim(trace_id, seq_index * tokens_here, tokens_here, 0)
    slots = jnp.arange(SEL)[None, :] < tile_count[:, None]
    tile_range = jnp.arange(seq_count * tiles_here)
    allowed = jnp.any(
        (key_tiles[:, :, None] == tile_range[None, None, :]) & slots[:, :, None], axis=1
    )

    qkv_all = lax.all_gather(
        jnp.stack([query_heads, key_heads, value_heads]), "seq", axis=1, tiled=True
    )
    grad_all = lax.all_gather(grad_heads, "seq", axis=0, tiled=True)
    stats = jnp.concatenate(
        [lse, delta, allowed.astype(jnp.float32).reshape(-1, tokens_here)], axis=0
    )
    stats_all = lax.all_gather(stats, "seq", axis=1, tiled=True)
    total_tokens = qkv_all.shape[1]
    lse_all = stats_all[:heads_here]
    delta_all = stats_all[heads_here:2 * heads_here]
    allowed_all = stats_all[2 * heads_here:].reshape(seq_count, tiles_here, -1)
    allowed_all = allowed_all.reshape(seq_count * tiles_here, -1)[:, : seq_count * tiles_here] > 0.5
    chunk = min(total_tokens, 2048)
    query_sum = None
    for first in range(0, total_tokens, chunk):
        listed = allowed[:, first // TILE:(first + chunk) // TILE]
        admit = jnp.repeat(jnp.repeat(listed, TILE, axis=0), TILE, axis=1) & (
            trace_here[:, None] != trace_id[None, first:first + chunk]
        )
        query_add = query_grads(
            query_heads, qkv_all[1, first:first + chunk], qkv_all[2, first:first + chunk],
            grad_heads, lse, delta, admit,
        )
        query_sum = query_add if query_sum is None else query_sum + query_add
    key_sum = None
    mine = seq_index * tiles_here
    for first in range(0, total_tokens, chunk):
        listed = lax.dynamic_slice_in_dim(allowed_all[first // TILE:(first + chunk) // TILE], mine, tiles_here, 1)
        admit = jnp.repeat(jnp.repeat(listed, TILE, axis=0), TILE, axis=1) & (
            trace_id[first:first + chunk, None] != trace_here[None, :]
        )
        key_add, value_add = key_grads(
            qkv_all[0, first:first + chunk], key_heads, value_heads, grad_all[first:first + chunk],
            lse_all[:, first:first + chunk], delta_all[:, first:first + chunk], admit,
        )
        if key_sum is None:
            key_sum, value_sum = key_add, value_add
        else:
            key_sum, value_sum = key_sum + key_add, value_sum + value_add
    d_query = query_sum.astype(jnp.bfloat16).reshape(tokens_here, width)
    d_key = key_sum.astype(jnp.bfloat16).reshape(tokens_here, width)
    d_value = value_sum.astype(jnp.bfloat16).reshape(tokens_here, width)
    contract = (((1,), (1,)), ((), ()))
    total = lax.dot_general(w_query, d_query, contract, preferred_element_type=jnp.float32)
    total = total + lax.dot_general(w_key, d_key, contract, preferred_element_type=jnp.float32)
    total = total + lax.dot_general(w_value, d_value, contract, preferred_element_type=jnp.float32)
    total = total.reshape((head_count, total.shape[0] // head_count) + total.shape[1:])
    total = total.astype(jnp.bfloat16)
    d_input = lax.all_to_all(total, "head", 0, 0, tiled=False).astype(jnp.float32).sum(axis=0)
    return d_input.T.astype(jnp.bfloat16)


def solution(mesh):
    in_specs = (
        P("seq", "head"),
        P("seq", "head"),
        P("seq", "head"),
        P("seq", "head"),
        P("seq", "head"),
        P("head", "seq"),
        P(),
        P("seq", None),
        P("seq"),
        P(None, "head"),
        P(None, "head"),
        P(None, "head"),
        P("head", None),
    )
    out_specs = P("seq", "head")
    return jax.shard_map(
        per_device, mesh=mesh, in_specs=in_specs, out_specs=out_specs, check_vma=False
    )
```

profile of v0, /device:TPU:32, one launch (start us, length us, event | category | flops | bytes accessed | tf_op | source)
XLA Modules:
  0.0 332.5 jit_solution(15955309985703991109)
XLA Ops:
  11.4 6.5 %collective-permute-start.4 = (bf16[512,128]{1,0:T(8,128)(2,1)}, bf16[512,128]{1,0:T(8,128)(2,1)S(1)}, u32[]{:S(2)}, u32[]{:S(2)}) collective-permute-start(bf16[512,128]{1,0:T(8,128)(2,1)} %param.17), channel_id=1, source_target_pairs={{0,5},{1,6},{2,7},{3,0},{4,1},{5,2},{6,3},{7,4},{8,13},{9,14},{10,... | collective-permute-start | bytes 393224 | tf_op jit(solution)/shard_map/ppermute | solution.py:13
  24.3 12.3 %collective-permute-done = bf16[512,128]{1,0:T(8,128)(2,1)S(1)} collective-permute-done((bf16[512,128]{1,0:T(8,128)(2,1)}, bf16[512,128]{1,0:T(8,128)(2,1)S(1)}, u32[]{:S(2)}, u32[]{:S(2)}) %collective-permute-start) | collective-permute-done | bytes 131104 | tf_op jit(solution)/shard_map/ppermute | solution.py:13
  43.5 11.0 %collective-permute-done.2 = bf16[512,128]{1,0:T(8,128)(2,1)S(1)} collective-permute-done((bf16[512,128]{1,0:T(8,128)(2,1)S(1)}, bf16[512,128]{1,0:T(8,128)(2,1)S(1)}, u32[]{:S(2)}, u32[]{:S(2)}) %collective-permute-start.2) | collective-permute-done | bytes 131104 | tf_op jit(solution)/shard_map/ppermute | solution.py:13
  60.9 38.2 %all_gather.10 = f32[3,16384]{1,0:T(4,128)S(1)} all-gather(f32[3,512]{1,0:T(4,128)S(1)} %pad_maximum_fusion.1), channel_id=1, replica_groups=mesh['seq'=32,'head'=8] {'seq'}, dimensions={1}, use_global_device_ids=true | all-gather | bytes 202752 | tf_op jit(solution)/shard_map/all_gather | solution.py:132
  99.9 7.8 %all-gather.4.cloned.1.call-done = bf16[3,16384,1,128]{3,1,2,0:T(8,128)(2,1)} async-done(((bf16[3,512,1,128]{3,1,2,0:T(8,128)(2,1)}), bf16[3,16384,1,128]{3,1,2,0:T(8,128)(2,1)}) %all-gather.4.cloned.1.call-update) | async-done | bytes 12582928 | tf_op jit(solution)/shard_map/all_gather | solution.py:125
  107.7 6.4 %broadcast_in_dim.238 = pred[2048,4,128]{2,1,0:T(4,128)(4,1)S(1)} broadcast(pred[2048,4]{1,0:T(8,128)(4,1)S(1)} %bitcast.407), dimensions={0,1} | broadcast | bytes 1056768 | tf_op jit(solution)/shard_map/broadcast_in_dim | solution.py:154
  114.1 4.1 %exponential_select_fusion.4 = f32[2048,512]{1,0:T(8,128)} fusion(pred[256,8,4,128]{3,2,1,0:T(4,128)(4,1)S(1)} %bitcast.399, bf16[512,128]{1,0:T(8,128)(2,1)S(1)} %copy-done.19, f32[2048]{0:T(1024)S(1)} %bitcast.458, s32[512]{0:T(512)S(1)} %dynamic_slice.27, s32[2048]{0:T(1024)S(1)} %get-tuple-element.32, ...), kind=kOutput, calls=%fused_computation.42 | convolution fusion | flops 273678336 | bytes 5916672 | tf_op jit(solution)/shard_map/rhd,chd->hrc/dot_general | solution.py:56
  118.3 6.4 %broadcast_in_dim.234 = pred[2048,4,128]{2,1,0:T(4,128)(4,1)S(1)} broadcast(pred[2048,4]{1,0:T(8,128)(4,1)S(1)} %bitcast.408), dimensions={0,1} | broadcast | bytes 1056768 | tf_op jit(solution)/shard_map/broadcast_in_dim | solution.py:154
  124.7 4.1 %exponential_select_fusion.6 = f32[2048,512]{1,0:T(8,128)} fusion(pred[256,8,4,128]{3,2,1,0:T(4,128)(4,1)S(1)} %bitcast.400, bf16[512,128]{1,0:T(8,128)(2,1)S(1)} %copy-done.19, f32[2048]{0:T(1024)S(1)} %bitcast.457, s32[512]{0:T(512)S(1)} %dynamic_slice.27, s32[2048]{0:T(1024)S(1)} %get-tuple-element.34, ...), kind=kOutput, calls=%fused_computation.46 | convolution fusion | flops 273678336 | bytes 5916672 | tf_op jit(solution)/shard_map/rhd,chd->hrc/dot_general | solution.py:56
  128.9 6.4 %broadcast_in_dim.242 = pred[2048,4,128]{2,1,0:T(4,128)(4,1)S(1)} broadcast(pred[2048,4]{1,0:T(8,128)(4,1)S(1)} %bitcast.409), dimensions={0,1} | broadcast | bytes 1056768 | tf_op jit(solution)/shard_map/broadcast_in_dim | solution.py:154
  135.3 4.0 %exponential_select_fusion.2 = f32[2048,512]{1,0:T(8,128)} fusion(pred[256,8,4,128]{3,2,1,0:T(4,128)(4,1)S(1)} %bitcast.401, bf16[512,128]{1,0:T(8,128)(2,1)S(1)} %copy-done.19, f32[2048]{0:T(1024)S(1)} %bitcast.456, s32[512]{0:T(512)S(1)} %dynamic_slice.27, s32[2048]{0:T(1024)S(1)} %get-tuple-element.30, ...), kind=kOutput, calls=%fused_computation.38 | convolution fusion | flops 273678336 | bytes 5916672 | tf_op jit(solution)/shard_map/rhd,chd->hrc/dot_general | solution.py:56
  139.4 6.4 %broadcast_in_dim.246 = pred[2048,4,128]{2,1,0:T(4,128)(4,1)S(1)} broadcast(pred[2048,4]{1,0:T(8,128)(4,1)S(1)} %bitcast.410), dimensions={0,1} | broadcast | bytes 1056768 | tf_op jit(solution)/shard_map/broadcast_in_dim | solution.py:154
  145.8 4.1 %exponential_select_fusion = f32[2048,512]{1,0:T(8,128)} fusion(pred[256,8,4,128]{3,2,1,0:T(4,128)(4,1)S(1)} %bitcast.402, bf16[512,128]{1,0:T(8,128)(2,1)S(1)} %copy-done.19, f32[2048]{0:T(1024)S(1)} %bitcast.455, s32[512]{0:T(512)S(1)} %dynamic_slice.27, s32[2048]{0:T(1024)S(1)} %get-tuple-element.29, ...), kind=kOutput, calls=%fused_computation.34 | convolution fusion | flops 273678336 | bytes 5916672 | tf_op jit(solution)/shard_map/rhd,chd->hrc/dot_general | solution.py:56
  149.9 6.4 %broadcast_in_dim.236 = pred[2048,4,128]{2,1,0:T(4,128)(4,1)S(1)} broadcast(pred[2048,4]{1,0:T(8,128)(4,1)S(1)} %bitcast.411), dimensions={0,1} | broadcast | bytes 1056768 | tf_op jit(solution)/shard_map/broadcast_in_dim | solution.py:154
  156.3 4.0 %exponential_select_fusion.5 = f32[2048,512]{1,0:T(8,128)} fusion(pred[256,8,4,128]{3,2,1,0:T(4,128)(4,1)S(1)} %bitcast.403, bf16[512,128]{1,0:T(8,128)(2,1)S(1)} %copy-done.19, f32[2048]{0:T(1024)S(1)} %bitcast.454, s32[512]{0:T(512)S(1)} %dynamic_slice.27, s32[2048]{0:T(1024)S(1)} %get-tuple-element.33, ...), kind=kOutput, calls=%fused_computation.44 | convolution fusion | flops 273678336 | bytes 5916672 | tf_op jit(solution)/shard_map/rhd,chd->hrc/dot_general | solution.py:56
  160.4 6.4 %broadcast_in_dim.231 = pred[2048,4,128]{2,1,0:T(4,128)(4,1)S(1)} broadcast(pred[2048,4]{1,0:T(8,128)(4,1)S(1)} %bitcast.412), dimensions={0,1} | broadcast | bytes 1056768 | tf_op jit(solution)/shard_map/broadcast_in_dim | solution.py:154
  166.9 4.2 %exponential_select_fusion.7 = f32[2048,512]{1,0:T(8,128)} fusion(pred[256,8,4,128]{3,2,1,0:T(4,128)(4,1)S(1)} %bitcast.404, bf16[512,128]{1,0:T(8,128)(2,1)S(1)} %copy-done.19, f32[2048]{0:T(1024)S(1)} %bitcast.453, s32[512]{0:T(512)S(1)} %dynamic_slice.27, s32[2048]{0:T(1024)S(1)} %get-tuple-element.35, ...), kind=kOutput, calls=%fused_computation.48 | convolution fusion | flops 273678336 | bytes 5916672 | tf_op jit(solution)/shard_map/rhd,chd->hrc/dot_general | solution.py:56
  171.9 3.9 %fusion.40 = f32[128,512]{1,0:T(8,128)S(1)} fusion(f32[2048,512]{1,0:T(8,128)} %exponential_select_fusion.7, bf16[512,128]{1,0:T(8,128)(2,1)S(1)} %copy-done.11, f32[2048]{0:T(1024)S(1)} %bitcast.434, bf16[3,16384,1,128]{3,1,2,0:T(8,128)(2,1)} %all-gather.4.cloned.1.call-done, bf16[16384,128]{0,1:T(8,128)(2,1)} %all-gather.6.cloned.1.call-done), kind=kOutput, calls=%fused_computation.82 | convolution fusion | flops 541065216 | bytes 5644288 | tf_op jit(solution)/shard_map/hrc,rhd->chd/dot_general | solution.py:67
  175.8 3.9 %fusion.55 = f32[128,512]{1,0:T(8,128)S(1)} fusion(f32[128,512]{1,0:T(8,128)S(1)} %fusion.40, f32[2048,512]{1,0:T(8,128)} %exponential_select_fusion.6, bf16[512,128]{1,0:T(8,128)(2,1)S(1)} %copy-done.11, f32[2048]{0:T(1024)S(1)} %bitcast.433, bf16[3,16384,1,128]{3,1,2,0:T(8,128)(2,1)} %all-gather.4.cloned.1.call-done, ...), kind=kOutput, calls=%fused_computation.97 | convolution fusion | flops 541130752 | bytes 5906432 | tf_op jit(solution)/shard_map/hrc,rhd->chd/dot_general | solution.py:67
  179.6 3.9 %fusion.54 = f32[128,512]{1,0:T(8,128)S(1)} fusion(f32[128,512]{1,0:T(8,128)S(1)} %fusion.55, f32[2048,512]{1,0:T(8,128)} %exponential_select_fusion.5, bf16[512,128]{1,0:T(8,128)(2,1)S(1)} %copy-done.11, f32[2048]{0:T(1024)S(1)} %bitcast.432, bf16[3,16384,1,128]{3,1,2,0:T(8,128)(2,1)} %all-gather.4.cloned.1.call-done, ...), kind=kOutput, calls=%fused_computation.96 | convolution fusion | flops 541130752 | bytes 5906432 | tf_op jit(solution)/shard_map/hrc,rhd->chd/dot_general | solution.py:67
  183.5 3.9 %fusion.53 = f32[128,512]{1,0:T(8,128)S(1)} fusion(f32[128,512]{1,0:T(8,128)S(1)} %fusion.54, f32[2048,512]{1,0:T(8,128)} %exponential_select_fusion.4, bf16[512,128]{1,0:T(8,128)(2,1)S(1)} %copy-done.11, f32[2048]{0:T(1024)S(1)} %bitcast.431, bf16[3,16384,1,128]{3,1,2,0:T(8,128)(2,1)} %all-gather.4.cloned.1.call-done, ...), kind=kOutput, calls=%fused_computation.95 | convolution fusion | flops 541130752 | bytes 5906432 | tf_op jit(solution)/shard_map/hrc,rhd->chd/dot_general | solution.py:67
  187.5 6.4 %broadcast_in_dim.240 = pred[2048,4,128]{2,1,0:T(4,128)(4,1)S(1)} broadcast(pred[2048,4]{1,0:T(8,128)(4,1)S(1)} %bitcast.413), dimensions={0,1} | broadcast | bytes 1056768 | tf_op jit(solution)/shard_map/broadcast_in_dim | solution.py:154
  193.9 4.0 %exponential_select_fusion.3 = f32[2048,512]{1,0:T(8,128)} fusion(pred[256,8,4,128]{3,2,1,0:T(4,128)(4,1)S(1)} %bitcast.405, bf16[512,128]{1,0:T(8,128)(2,1)S(1)} %copy-done.19, f32[2048]{0:T(1024)S(1)} %bitcast.452, s32[512]{0:T(512)S(1)} %dynamic_slice.27, s32[2048]{0:T(1024)S(1)} %get-tuple-element.31, ...), kind=kOutput, calls=%fused_computation.40 | convolution fusion | flops 273678336 | bytes 5916672 | tf_op jit(solution)/shard_map/rhd,chd->hrc/dot_general | solution.py:56
  197.9 3.9 %fusion.52 = f32[128,512]{1,0:T(8,128)S(1)} fusion(f32[128,512]{1,0:T(8,128)S(1)} %fusion.53, f32[2048,512]{1,0:T(8,128)} %exponential_select_fusion.3, bf16[512,128]{1,0:T(8,128)(2,1)S(1)} %copy-done.11, f32[2048]{0:T(1024)S(1)} %bitcast.430, bf16[3,16384,1,128]{3,1,2,0:T(8,128)(2,1)} %all-gather.4.cloned.1.call-done, ...), kind=kOutput, calls=%fused_computation.94 | convolution fusion | flops 541130752 | bytes 5906432 | tf_op jit(solution)/shard_map/hrc,rhd->chd/dot_general | solution.py:67
  201.8 3.9 %fusion.51 = f32[128,512]{1,0:T(8,128)S(1)} fusion(f32[128,512]{1,0:T(8,128)S(1)} %fusion.52, f32[2048,512]{1,0:T(8,128)} %exponential_select_fusion.2, bf16[512,128]{1,0:T(8,128)(2,1)S(1)} %copy-done.11, f32[2048]{0:T(1024)S(1)} %bitcast.429, bf16[3,16384,1,128]{3,1,2,0:T(8,128)(2,1)} %all-gather.4.cloned.1.call-done, ...), kind=kOutput, calls=%fused_computation.93 | convolution fusion | flops 541130752 | bytes 5906432 | tf_op jit(solution)/shard_map/hrc,rhd->chd/dot_general | solution.py:67
  205.8 6.4 %broadcast_in_dim.244 = pred[2048,4,128]{2,1,0:T(4,128)(4,1)S(1)} broadcast(pred[2048,4]{1,0:T(8,128)(4,1)S(1)} %bitcast.414), dimensions={0,1} | broadcast | bytes 1056768 | tf_op jit(solution)/shard_map/broadcast_in_dim | solution.py:154
  212.2 4.3 %exponential_select_fusion.1 = f32[2048,512]{1,0:T(8,128)} fusion(pred[256,8,4,128]{3,2,1,0:T(4,128)(4,1)S(1)} %bitcast.406, bf16[512,128]{1,0:T(8,128)(2,1)S(1)} %copy-done.19, f32[2048]{0:T(1024)S(1)} %bitcast.451, s32[512]{0:T(512)S(1)} %dynamic_slice.27, s32[2048]{0:T(1024)S(1)} %get-tuple-element.36, ...), kind=kOutput, calls=%fused_computation.36 | convolution fusion | flops 273678336 | bytes 5916672 | tf_op jit(solution)/shard_map/rhd,chd->hrc/dot_general | solution.py:56
  216.4 3.9 %fusion.50 = f32[128,512]{1,0:T(8,128)S(1)} fusion(f32[128,512]{1,0:T(8,128)S(1)} %fusion.51, f32[2048,512]{1,0:T(8,128)} %exponential_select_fusion.1, bf16[512,128]{1,0:T(8,128)(2,1)S(1)} %copy-done.11, f32[2048]{0:T(1024)S(1)} %bitcast.428, bf16[3,16384,1,128]{3,1,2,0:T(8,128)(2,1)} %all-gather.4.cloned.1.call-done, ...), kind=kOutput, calls=%fused_computation.92 | convolution fusion | flops 541130752 | bytes 5906432 | tf_op jit(solution)/shard_map/hrc,rhd->chd/dot_general | solution.py:67
  220.3 3.9 %fusion.87 = bf16[512,128]{0,1:T(8,128)(2,1)S(1)} fusion(f32[128,512]{1,0:T(8,128)S(1)} %fusion.50, f32[2048,512]{1,0:T(8,128)} %exponential_select_fusion, bf16[512,128]{1,0:T(8,128)(2,1)S(1)} %copy-done.11, f32[2048]{0:T(1024)S(1)} %bitcast.427, bf16[3,16384,1,128]{3,1,2,0:T(8,128)(2,1)} %all-gather.4.cloned.1.call-done, ...), kind=kOutput, calls=%fused_computation.119 | convolution fusion | flops 541196288 | bytes 5775360 | tf_op jit(solution)/shard_map/hrc,rhd->chd/dot_general | solution.py:67
  276.8 4.2 %fusion.86 = f32[512,1024]{1,0:T(8,128)} fusion(bf16[1024,128]{1,0:T(8,128)(2,1)S(1)} %copy-done.15, f32[128,512]{1,0:T(8,128)S(1)} %convolution_add_fusion.1, bf16[512,2048]{0,1:T(8,128)(2,1)} %fusion.2, bf16[3,16384,1,128]{3,1,2,0:T(8,128)(2,1)} %all-gather.4.cloned.1.call-done), kind=kOutput, calls=%fused_computation.118 | convolution fusion | flops 402784256 | bytes 5242880 | tf_op jit(solution)/shard_map/dot_general | solution.py:169
  281.0 4.1 %fusion.48 = bf16[64,8,8,128]{3,2,1,0:T(8,128)(2,1)S(1)} fusion(bf16[1024,128]{1,0:T(8,128)(2,1)} %param.24, f32[512,1024]{1,0:T(8,128)} %fusion.86, f32[512,1024]{1,0:T(8,128)S(1)} %copy-done.13, f32[128,512]{1,0:T(8,128)} %fusion.71, f32[2048,512]{1,0:T(8,128)} %exponential_select_fusion, bf16[16384,128]{0,1:T(8,128)(2,1)} %all-gather.6.cloned.1.call-done), kind=kOutput, calls=%fused_computation.90 | convolution fusion | flops 405405696 | bytes 10485760 | tf_op jit(solution)/shard_map/dot_general | solution.py:171
  285.3 39.1 %all_to_all.5 = bf16[8,128,512]{1,2,0:T(8,128)(2,1)S(1)} all-to-all(bf16[8,128,512]{1,2,0:T(8,128)(2,1)S(1)} %bitcast.398), channel_id=1, replica_groups=mesh['seq'=32,'head'=8] {'head'}, dimensions={0} | all-to-all | bytes 2097152 | tf_op jit(solution)/shard_map/all_to_all | solution.py:174
  (168 shorter events, 79.5 us)
Async XLA Ops:
  6.5 217.6 %copy-start = (bf16[1024,128]{1,0:T(8,128)(2,1)S(1)}, bf16[1024,128]{1,0:T(8,128)(2,1)}, u32[]{:S(2)}) copy-start(bf16[1024,128]{1,0:T(8,128)(2,1)} %param.23) | copy-start | bytes 786436
  6.5 30.1 %copy-start.18 = (bf16[512,128]{1,0:T(8,128)(2,1)S(1)}, bf16[512,128]{1,0:T(8,128)(2,1)}, u32[]{:S(2)}) copy-start(bf16[512,128]{1,0:T(8,128)(2,1)} %param.17) | copy-start | bytes 393220
  6.5 17.6 %copy-start.17 = (bf16[512,128]{1,0:T(8,128)(2,1)S(1)}, bf16[512,128]{1,0:T(8,128)(2,1)}, u32[]{:S(2)}) copy-start(bf16[512,128]{1,0:T(8,128)(2,1)} %param.16) | copy-start | bytes 393220
  6.5 52.3 %copy-start.22 = (s32[4]{0:T(128)S(1)}, s32[4]{0:T(128)}, u32[]{:S(2)}) copy-start(s32[4]{0:T(128)} %param.21) | copy-start | bytes 52
  6.5 52.4 %copy-start.21 = (s32[4,48]{1,0:T(4,128)S(1)}, s32[4,48]{1,0:T(4,128)}, u32[]{:S(2)}) copy-start(s32[4,48]{1,0:T(4,128)} %param.20) | copy-start | bytes 2308
  6.5 54.2 %copy-start.20 = (s32[16384]{0:T(1024)S(1)}, s32[16384]{0:T(1024)}, u32[]{:S(2)}) copy-start(s32[16384]{0:T(1024)} %param.19) | copy-start | bytes 196612
  6.6 54.3 %copy-start.16 = (f32[1,512]{1,0:T(1,128)S(1)}, f32[1,512]{1,0:T(1,128)}, u32[]{:S(2)}) copy-start(f32[1,512]{1,0:T(1,128)} %param.18) | copy-start | bytes 6148
  6.6 101.1 %all-gather.4.cloned.1.call-start = ((), (), s32[]{:S(2)}) async-start(), calls=%async_computation.1 | async-start | bytes 12976128 | tf_op jit(solution)/shard_map/all_gather | solution.py:125
  8.5 163.4 %all-gather.6.cloned.1.call-start = ((), (), s32[]{:S(2)}) async-start(), calls=%async_computation.2 | async-start | bytes 4325376 | tf_op jit(solution)/shard_map/all_gather | solution.py:128
  8.6 46.0 %collective-permute-start.5 = (bf16[512,128]{1,0:T(8,128)(2,1)}, bf16[512,128]{1,0:T(8,128)(2,1)S(1)}, u32[]{:S(2)}, u32[]{:S(2)}) collective-permute-start(bf16[512,128]{1,0:T(8,128)(2,1)} %param.17), channel_id=1, source_target_pairs={{0,6},{1,7},{2,0},{3,1},{4,2},{5,3},{6,4},{7,5},{8,14},{9,15},{10,... | collective-permute-start | bytes 393224 | tf_op jit(solution)/shard_map/ppermute | solution.py:13
  11.4 43.1 %collective-permute-start.4 = (bf16[512,128]{1,0:T(8,128)(2,1)}, bf16[512,128]{1,0:T(8,128)(2,1)S(1)}, u32[]{:S(2)}, u32[]{:S(2)}) collective-permute-start(bf16[512,128]{1,0:T(8,128)(2,1)} %param.17), channel_id=1, source_target_pairs={{0,5},{1,6},{2,7},{3,0},{4,1},{5,2},{6,3},{7,4},{8,13},{9,14},{10,... | collective-permute-start | bytes 393224 | tf_op jit(solution)/shard_map/ppermute | solution.py:13
  17.9 36.6 %collective-permute-start.3 = (bf16[512,128]{1,0:T(8,128)(2,1)}, bf16[512,128]{1,0:T(8,128)(2,1)S(1)}, u32[]{:S(2)}, u32[]{:S(2)}) collective-permute-start(bf16[512,128]{1,0:T(8,128)(2,1)} %param.17), channel_id=1, source_target_pairs={{0,4},{1,5},{2,6},{3,7},{4,0},{5,1},{6,2},{7,3},{8,12},{9,13},{10,... | collective-permute-start | bytes 393224 | tf_op jit(solution)/shard_map/ppermute | solution.py:13
  20.7 19.5 %collective-permute-start.1 = (bf16[512,128]{1,0:T(8,128)(2,1)}, bf16[512,128]{1,0:T(8,128)(2,1)S(1)}, u32[]{:S(2)}, u32[]{:S(2)}) collective-permute-start(bf16[512,128]{1,0:T(8,128)(2,1)} %param.17), channel_id=1, source_target_pairs={{0,2},{1,3},{2,4},{3,5},{4,6},{5,7},{6,0},{7,1},{8,10},{9,11},{10,... | collective-permute-start | bytes 393224 | tf_op jit(solution)/shard_map/ppermute | solution.py:13
  20.7 15.9 %collective-permute-start = (bf16[512,128]{1,0:T(8,128)(2,1)}, bf16[512,128]{1,0:T(8,128)(2,1)S(1)}, u32[]{:S(2)}, u32[]{:S(2)}) collective-permute-start(bf16[512,128]{1,0:T(8,128)(2,1)} %param.17), channel_id=1, source_target_pairs={{0,1},{1,2},{2,3},{3,4},{4,5},{5,6},{6,7},{7,0},{8,9},{9,10},{10,1... | collective-permute-start | bytes 393224 | tf_op jit(solution)/shard_map/ppermute | solution.py:13
  22.0 92.1 %copy-start.19 = (bf16[512,128]{1,0:T(8,128)(2,1)S(1)}, bf16[512,128]{1,0:T(8,128)(2,1)}, u32[]{:S(2)}) copy-start(bf16[512,128]{1,0:T(8,128)(2,1)} %param.14) | copy-start | bytes 393220
  36.6 17.8 %collective-permute-start.2 = (bf16[512,128]{1,0:T(8,128)(2,1)S(1)}, bf16[512,128]{1,0:T(8,128)(2,1)S(1)}, u32[]{:S(2)}, u32[]{:S(2)}) collective-permute-start(bf16[512,128]{1,0:T(8,128)(2,1)S(1)} %copy-done.18), channel_id=1, source_target_pairs={{0,3},{1,4},{2,5},{3,6},{4,7},{5,0},{6,1},{7,2},{8,11},{9,12},{10,... | collective-permute-start | bytes 393224 | tf_op jit(solution)/shard_map/ppermute | solution.py:13
  40.1 17.5 %collective-permute-start.6 = (bf16[512,128]{1,0:T(8,128)(2,1)S(1)}, bf16[512,128]{1,0:T(8,128)(2,1)S(1)}, u32[]{:S(2)}, u32[]{:S(2)}) collective-permute-start(bf16[512,128]{1,0:T(8,128)(2,1)S(1)} %copy-done.18), channel_id=1, source_target_pairs={{0,7},{1,0},{2,1},{3,2},{4,3},{5,4},{6,5},{7,6},{8,15},{9,8},{10,9... | collective-permute-start | bytes 393224 | tf_op jit(solution)/shard_map/ppermute | solution.py:13
  166.8 5.0 %copy-start.11 = (bf16[512,128]{1,0:T(8,128)(2,1)S(1)}, bf16[512,128]{1,0:T(8,128)(2,1)}, u32[]{:S(2)}) copy-start(bf16[512,128]{1,0:T(8,128)(2,1)} %param.15) | copy-start | bytes 393220
  224.2 5.4 %copy-start.5 = (f32[2048,512]{1,0:T(8,128)S(1)}, f32[2048,512]{1,0:T(8,128)}, u32[]{:S(2)}) copy-start(f32[2048,512]{1,0:T(8,128)} %exponential_select_fusion.5) | copy-start | bytes 12582916
  224.2 8.4 %copy-start.6 = (f32[2048,512]{1,0:T(8,128)S(1)}, f32[2048,512]{1,0:T(8,128)}, u32[]{:S(2)}) copy-start(f32[2048,512]{1,0:T(8,128)} %exponential_select_fusion.3) | copy-start | bytes 12582916
  226.0 9.0 %copy-start.9 = (f32[2048,512]{1,0:T(8,128)S(1)}, f32[2048,512]{1,0:T(8,128)}, u32[]{:S(2)}) copy-start(f32[2048,512]{1,0:T(8,128)} %exponential_select_fusion.1) | copy-start | bytes 12582916
  226.0 14.4 %slice-start = ((s8[12582912]{0:T(1024)(128)(4,1)}), s8[4194304]{0:T(1024)(128)(4,1)S(1)}, s32[]{:S(2)}) async-start(s8[12582912]{0:T(1024)(128)(4,1)} %bitcast.394), calls=%async_computation.3 | async-start | bytes 8388608
  229.6 10.8 %slice-start.1 = ((s8[12582912]{0:T(1024)(128)(4,1)}), s8[4194304]{0:T(1024)(128)(4,1)S(1)}, s32[]{:S(2)}) async-start(s8[12582912]{0:T(1024)(128)(4,1)} %bitcast.394), calls=%async_computation.4 | async-start | bytes 8388608
  232.6 4.0 %copy-start.12 = (bf16[512,128]{1,0:T(8,128)(2,1)S(1)}, bf16[512,128]{1,0:T(8,128)(2,1)}, u32[]{:S(2)}) copy-start(bf16[512,128]{1,0:T(8,128)(2,1)} %param.13) | copy-start | bytes 393220
  234.9 5.4 %slice-start.2 = ((s8[12582912]{0:T(1024)(128)(4,1)}), s8[4194304]{0:T(1024)(128)(4,1)S(1)}, s32[]{:S(2)}) async-start(s8[12582912]{0:T(1024)(128)(4,1)} %bitcast.394), calls=%async_computation.5 | async-start | bytes 8388608
  247.4 5.3 %copy-start.4 = (f32[2048,512]{1,0:T(8,128)S(1)}, f32[2048,512]{1,0:T(8,128)}, u32[]{:S(2)}) copy-start(f32[2048,512]{1,0:T(8,128)} %exponential_select_fusion.7) | copy-start | bytes 12582916
  250.5 4.0 %copy-start.2 = (f32[2048,512]{1,0:T(8,128)S(1)}, f32[2048,512]{1,0:T(8,128)}, u32[]{:S(2)}) copy-start(f32[2048,512]{1,0:T(8,128)} %exponential_select_fusion.4) | copy-start | bytes 12582916
  250.5 4.0 %copy-start.14 = (f32[128,512]{1,0:T(8,128)S(1)}, f32[128,512]{1,0:T(8,128)}, u32[]{:S(2)}) copy-start(f32[128,512]{1,0:T(8,128)} %fusion.30) | copy-start | bytes 786436
  252.8 3.5 %copy-start.3 = (f32[2048,512]{1,0:T(8,128)S(1)}, f32[2048,512]{1,0:T(8,128)}, u32[]{:S(2)}) copy-start(f32[2048,512]{1,0:T(8,128)} %exponential_select_fusion.2) | copy-start | bytes 12582916
  254.6 4.0 %copy-start.8 = (f32[2048,512]{1,0:T(8,128)S(1)}, f32[2048,512]{1,0:T(8,128)}, u32[]{:S(2)}) copy-start(f32[2048,512]{1,0:T(8,128)} %fusion.98) | copy-start | bytes 12582916
  276.3 4.7 %copy-start.13 = (f32[512,1024]{1,0:T(8,128)S(1)}, f32[512,1024]{1,0:T(8,128)}, u32[]{:S(2)}) copy-start(f32[512,1024]{1,0:T(8,128)} %fusion.140) | copy-start | bytes 6291460
  281.0 44.3 %copy-start.1 = (bf16[1024,128]{1,0:T(8,128)(2,1)S(1)}, bf16[1024,128]{1,0:T(8,128)(2,1)}, u32[]{:S(2)}) copy-start(bf16[1024,128]{1,0:T(8,128)(2,1)} %param.23) | copy-start | bytes 786436
  (3 other events, 6.1 us)
Sparse Core Ops, SparseCore 0:
  9.2 98.3 all-gather.3
  109.5 62.3 all-gather.5
where the time goes:
time: 338 us; the launch traced here: 332 us
  matrix products  125 us (37%)
  blocking collectives  77.4 us (23%)
  local copies, waits for them, and re-layouts  57.8 us (17%)
  waiting for transfers between devices  34.9 us (10%)
  starting transfers between devices  19 us (6%)
  between operations  14.8 us (4%)
    broadcast_in_dim x8, local copies, waits for them, and re-layouts, per_device(): jnp.repeat(jnp.repeat(listed, TILE, axis=0), TILE, axis=1)  51.1 us
    all_to_all x1, blocking collectives, per_device(): lax.all_to_all(total, 'head', 0, 0, tiled=False).astype(jnp.float32)  39.1 us
    all_gather x1, blocking collectives, per_device(): stats_all = lax.all_gather(stats, 'seq', axis=1, tiled=True)  38.2 us
    dot_general x8, matrix products, key_grads(): jnp.einsum('rhd,chd->hrc', query_heads, key_heads, preferred_element_type...  32.9 us
    dot_general x8, matrix products, key_grads(): jnp.einsum('hrc,rhd->chd', score_grad, query_heads, preferred_element_typ...  31 us
    ppermute x7, waiting for transfers between devices, from_behind(): lax.ppermute(value, axis, [(i, (i + by) % count) for i in range(count)])  26.3 us
    ppermute x7, starting transfers between devices, from_behind(): lax.ppermute(value, axis, [(i, (i + by) % count) for i in range(count)])  18.9 us
    dot_general x8, matrix products, query_grads(): jnp.einsum('rhd,chd->hrc', grad_heads, value_heads, preferred_element_typ...  18.3 us
  transfers between devices with their start and end apart: 9, of which 5 were waited for; matrix products, arithmetic and copies ran while one was open for 21% of the time, Pallas kernels for 0%

commit v1 on v0

--- a/solution.py
+++ b/solution.py
@@ -50,22 +50,22 @@
     return jnp.einsum("hrc,chd->rhd", score_grad, key_heads, preferred_element_type=jnp.float32)
 
 
-def key_grads(query_heads, key_heads, value_heads, grad_heads, norm_rows, delta_rows, admit):
+def key_grads(query_heads, key_heads, value_heads, grad_heads, norm_cols, delta_cols, admit):
     scale = query_heads.shape[-1] ** (-0.5)
     scores = (
-        jnp.einsum("rhd,chd->hrc", query_heads, key_heads, preferred_element_type=jnp.float32)
+        jnp.einsum("chd,rhd->hcr", key_heads, query_heads, preferred_element_type=jnp.float32)
         * scale
     )
-    probs = jnp.where(admit[None], jnp.exp(scores - norm_rows[:, :, None]), 0.0)
+    probs = jnp.where(admit[None], jnp.exp(scores - norm_cols[:, None, :]), 0.0)
     value_grad = jnp.einsum(
-        "hrc,rhd->chd", probs.astype(jnp.bfloat16), grad_heads, preferred_element_type=jnp.float32
+        "hcr,rhd->chd", probs.astype(jnp.bfloat16), grad_heads, preferred_element_type=jnp.float32
     )
     prob_grad = jnp.einsum(
-        "rhd,chd->hrc", grad_heads, value_heads, preferred_element_type=jnp.float32
+        "chd,rhd->hcr", value_heads, grad_heads, preferred_element_type=jnp.float32
     )
-    score_grad = (probs * (prob_grad - delta_rows[:, :, None]) * scale).astype(jnp.bfloat16)
+    score_grad = (probs * (prob_grad - delta_cols[:, None, :]) * scale).astype(jnp.bfloat16)
     key_grad = jnp.einsum(
-        "hrc,rhd->chd", score_grad, query_heads, preferred_element_type=jnp.float32
+        "hcr,rhd->chd", score_grad, query_heads, preferred_element_type=jnp.float32
     )
     return (key_grad, value_grad)
 
@@ -151,8 +151,8 @@
     mine = seq_index * tiles_here
     for first in range(0, total_tokens, chunk):
         listed = lax.dynamic_slice_in_dim(allowed_all[first // TILE:(first + chunk) // TILE], mine, tiles_here, 1)
-        admit = jnp.repeat(jnp.repeat(listed, TILE, axis=0), TILE, axis=1) & (
-            trace_id[first:first + chunk, None] != trace_here[None, :]
+        admit = jnp.repeat(jnp.repeat(listed.T, TILE, axis=0), TILE, axis=1) & (
+            trace_here[:, None] != trace_id[None, first:first + chunk]
         )
         key_add, value_add = key_grads(
             qkv_all[0, first:first + chunk], key_heads, value_heads, grad_all[first:first + chunk],

time: 338 us -> 321 us (0.950)
  local copies, waits for them, and re-layouts: 57.8 us -> 7.64 us
  waiting for transfers between devices: 34.9 us -> 62 us
  matrix products: 125 us -> 131 us
    broadcast_in_dim x8, local copies, waits for them, and re-layouts: 51.1 us -> 0.66 us  [per_device(): jnp.repeat(listed.T, TILE, axis=0)]
    all_gather x1, waiting for transfers between devices: 0.79 us -> 32.4 us  [per_device(): grad_all = lax.all_gather(grad_heads, 'seq', axis=0, tiled=True)]
    ppermute x7, waiting for transfers between devices: 26.3 us -> 15.8 us  [from_behind(): lax.ppermute(value, axis, [(i, (i + by) % count) for i in range(count)])]
    all_gather x1, waiting for transfers between devices: 7.77 us -> 13.7 us  [per_device(): lax.all_gather(jnp.stack([query_heads, key_heads, value_heads]), 'seq', a...]
  transfers between devices with their start and end apart: 9 -> 9, of which waited for: 5 -> 5; matrix products, arithmetic and copies ran while one was open for 21% -> 13% of each run, Pallas kernels for 0% -> 0%
where the time goes in v1:
time: 321 us; the launch traced here: 315 us
  matrix products  131 us (41%)
  blocking collectives  75.7 us (24%)
  waiting for transfers between devices  62 us (19%)
  starting transfers between devices  20.7 us (6%)
  between operations  14.5 us (5%)
  local copies, waits for them, and re-layouts  7.64 us (2%)
  other arithmetic  3.34 us (1%)
    all_to_all x1, blocking collectives, per_device(): lax.all_to_all(total, 'head', 0, 0, tiled=False).astype(jnp.float32)  38.8 us
    all_gather x1, blocking collectives, per_device(): stats_all = lax.all_gather(stats, 'seq', axis=1, tiled=True)  36.8 us
    dot_general x8, matrix products, key_grads(): jnp.einsum('chd,rhd->hcr', key_heads, query_heads, preferred_element_type...  35.6 us
    all_gather x1, waiting for transfers between devices, per_device(): grad_all = lax.all_gather(grad_heads, 'seq', axis=0, tiled=True)  32.4 us
    dot_general x8, matrix products, key_grads(): jnp.einsum('hcr,rhd->chd', score_grad, query_heads, preferred_element_typ...  31.4 us
    ppermute x7, starting transfers between devices, from_behind(): lax.ppermute(value, axis, [(i, (i + by) % count) for i in range(count)])  20.6 us
    dot_general x8, matrix products, query_grads(): jnp.einsum('rhd,chd->hrc', grad_heads, value_heads, preferred_element_typ...  20 us
    ppermute x7, waiting for transfers between devices, from_behind(): lax.ppermute(value, axis, [(i, (i + by) % count) for i in range(count)])  15.8 us
  transfers between devices with their start and end apart: 9, of which 5 were waited for; matrix products, arithmetic and copies ran while one was open for 13% of the time, Pallas kernels for 0%

profile of v1, /device:TPU:32, one launch (start us, length us, event | category | flops | bytes accessed | tf_op | source)
XLA Modules:
  0.0 315.1 jit_solution(18162008896455827793)
XLA Ops:
  8.6 6.4 %collective-permute-start = (bf16[512,128]{1,0:T(8,128)(2,1)}, bf16[512,128]{1,0:T(8,128)(2,1)S(1)}, u32[]{:S(2)}, u32[]{:S(2)}) collective-permute-start(bf16[512,128]{1,0:T(8,128)(2,1)} %param.17), channel_id=1, source_target_pairs={{0,1},{1,2},{2,3},{3,4},{4,5},{5,6},{6,7},{7,0},{8,9},{9,10},{10,1... | collective-permute-start | bytes 393224 | tf_op jit(solution)/shard_map/ppermute | solution.py:13
  19.7 7.9 %collective-permute-start.4 = (bf16[512,128]{1,0:T(8,128)(2,1)}, bf16[512,128]{1,0:T(8,128)(2,1)S(1)}, u32[]{:S(2)}, u32[]{:S(2)}) collective-permute-start(bf16[512,128]{1,0:T(8,128)(2,1)} %param.17), channel_id=1, source_target_pairs={{0,5},{1,6},{2,7},{3,0},{4,1},{5,2},{6,3},{7,4},{8,13},{9,14},{10,... | collective-permute-start | bytes 393224 | tf_op jit(solution)/shard_map/ppermute | solution.py:13
  35.3 6.2 %collective-permute-done.4 = bf16[512,128]{1,0:T(8,128)(2,1)S(1)} collective-permute-done((bf16[512,128]{1,0:T(8,128)(2,1)}, bf16[512,128]{1,0:T(8,128)(2,1)S(1)}, u32[]{:S(2)}, u32[]{:S(2)}) %collective-permute-start.4) | collective-permute-done | bytes 131104 | tf_op jit(solution)/shard_map/ppermute | solution.py:13
  41.6 8.1 %collective-permute-done.6 = bf16[512,128]{1,0:T(8,128)(2,1)S(1)} collective-permute-done((bf16[512,128]{1,0:T(8,128)(2,1)S(1)}, bf16[512,128]{1,0:T(8,128)(2,1)S(1)}, u32[]{:S(2)}, u32[]{:S(2)}) %collective-permute-start.6) | collective-permute-done | bytes 131104 | tf_op jit(solution)/shard_map/ppermute | solution.py:13
  53.0 36.8 %all_gather.10 = f32[3,16384]{1,0:T(4,128)S(1)} all-gather(f32[3,512]{1,0:T(4,128)S(1)} %pad_maximum_fusion.1), channel_id=1, replica_groups=mesh['seq'=32,'head'=8] {'seq'}, dimensions={1}, use_global_device_ids=true | all-gather | bytes 202752 | tf_op jit(solution)/shard_map/all_gather | solution.py:132
  91.5 13.7 %all-gather.4.cloned.1.call-done = bf16[3,16384,1,128]{3,1,2,0:T(8,128)(2,1)} async-done(((bf16[3,512,1,128]{3,1,2,0:T(8,128)(2,1)}), bf16[3,16384,1,128]{3,1,2,0:T(8,128)(2,1)}) %all-gather.4.cloned.1.call-update) | async-done | bytes 12582928 | tf_op jit(solution)/shard_map/all_gather | solution.py:125
  105.2 4.5 %bitcast_select_fusion.5 = f32[512,2048]{0,1:T(8,128)} fusion(bf16[512,128]{1,0:T(8,128)(2,1)S(1)} %copy-done.10, f32[2048]{0:T(1024)S(1)} %bitcast.540, s32[512]{0:T(512)S(1)} %dynamic_slice.27, s32[2048]{0:T(1024)S(1)} %get-tuple-element.33, pred[512,16]{0,1:T(8,128)(4,1)S(1)} %bitcast.549, bf16[3,16384,1,128]{3,1,2,0:T(8,128)(2,1)} %all-gather.4.cloned.1.call-done), kind=kOutput, calls=%fused_computation.40 | convolution fusion | flops 273678336 | bytes 4876288 | tf_op jit(solution)/shard_map/chd,rhd->hcr/dot_general | solution.py:56
  109.6 4.5 %bitcast_select_fusion.6 = f32[512,2048]{0,1:T(8,128)} fusion(bf16[512,128]{1,0:T(8,128)(2,1)S(1)} %copy-done.10, f32[2048]{0:T(1024)S(1)} %bitcast.539, s32[512]{0:T(512)S(1)} %dynamic_slice.27, s32[2048]{0:T(1024)S(1)} %get-tuple-element.34, pred[512,16]{0,1:T(8,128)(4,1)S(1)} %bitcast.551, bf16[3,16384,1,128]{3,1,2,0:T(8,128)(2,1)} %all-gather.4.cloned.1.call-done), kind=kOutput, calls=%fused_computation.44 | convolution fusion | flops 273678336 | bytes 4876288 | tf_op jit(solution)/shard_map/chd,rhd->hcr/dot_general | solution.py:56
  114.2 4.5 %bitcast_select_fusion.7 = f32[512,2048]{0,1:T(8,128)} fusion(bf16[512,128]{1,0:T(8,128)(2,1)S(1)} %copy-done.10, f32[2048]{0:T(1024)S(1)} %bitcast.538, s32[512]{0:T(512)S(1)} %dynamic_slice.27, s32[2048]{0:T(1024)S(1)} %get-tuple-element.35, pred[512,16]{0,1:T(8,128)(4,1)S(1)} %bitcast.552, bf16[3,16384,1,128]{3,1,2,0:T(8,128)(2,1)} %all-gather.4.cloned.1.call-done), kind=kOutput, calls=%fused_computation.48 | convolution fusion | flops 273678336 | bytes 4876288 | tf_op jit(solution)/shard_map/chd,rhd->hcr/dot_general | solution.py:56
  118.6 4.4 %bitcast_select_fusion.3 = f32[512,2048]{0,1:T(8,128)} fusion(bf16[512,128]{1,0:T(8,128)(2,1)S(1)} %copy-done.10, f32[2048]{0:T(1024)S(1)} %bitcast.537, s32[512]{0:T(512)S(1)} %dynamic_slice.27, s32[2048]{0:T(1024)S(1)} %get-tuple-element.31, pred[512,16]{0,1:T(8,128)(4,1)S(1)} %bitcast.553, bf16[3,16384,1,128]{3,1,2,0:T(8,128)(2,1)} %all-gather.4.cloned.1.call-done), kind=kOutput, calls=%fused_computation.32 | convolution fusion | flops 273678336 | bytes 4876288 | tf_op jit(solution)/shard_map/chd,rhd->hcr/dot_general | solution.py:56
  123.1 4.5 %bitcast_select_fusion.4 = f32[512,2048]{0,1:T(8,128)} fusion(bf16[512,128]{1,0:T(8,128)(2,1)S(1)} %copy-done.10, f32[2048]{0:T(1024)S(1)} %bitcast.536, s32[512]{0:T(512)S(1)} %dynamic_slice.27, s32[2048]{0:T(1024)S(1)} %get-tuple-element.32, pred[512,16]{0,1:T(8,128)(4,1)S(1)} %bitcast.554, bf16[3,16384,1,128]{3,1,2,0:T(8,128)(2,1)} %all-gather.4.cloned.1.call-done), kind=kOutput, calls=%fused_computation.36 | convolution fusion | flops 273678336 | bytes 4876288 | tf_op jit(solution)/shard_map/chd,rhd->hcr/dot_general | solution.py:56
  127.5 4.5 %bitcast_select_fusion.1 = f32[512,2048]{0,1:T(8,128)} fusion(bf16[512,128]{1,0:T(8,128)(2,1)S(1)} %copy-done.10, f32[2048]{0:T(1024)S(1)} %bitcast.535, s32[512]{0:T(512)S(1)} %dynamic_slice.27, s32[2048]{0:T(1024)S(1)} %get-tuple-element.36, pred[512,16]{0,1:T(8,128)(4,1)S(1)} %bitcast.555, bf16[3,16384,1,128]{3,1,2,0:T(8,128)(2,1)} %all-gather.4.cloned.1.call-done), kind=kOutput, calls=%fused_computation.24 | convolution fusion | flops 273678336 | bytes 4876288 | tf_op jit(solution)/shard_map/chd,rhd->hcr/dot_general | solution.py:56
  132.0 4.4 %bitcast_select_fusion.2 = f32[512,2048]{0,1:T(8,128)} fusion(bf16[512,128]{1,0:T(8,128)(2,1)S(1)} %copy-done.10, f32[2048]{0:T(1024)S(1)} %bitcast.534, s32[512]{0:T(512)S(1)} %dynamic_slice.27, s32[2048]{0:T(1024)S(1)} %get-tuple-element.30, pred[512,16]{0,1:T(8,128)(4,1)S(1)} %bitcast.556, bf16[3,16384,1,128]{3,1,2,0:T(8,128)(2,1)} %all-gather.4.cloned.1.call-done), kind=kOutput, calls=%fused_computation.28 | convolution fusion | flops 273678336 | bytes 4876288 | tf_op jit(solution)/shard_map/chd,rhd->hcr/dot_general | solution.py:56
  136.4 32.4 %all-gather.6.cloned.1.call-done = bf16[16384,128]{0,1:T(8,128)(2,1)} async-done(((bf16[512,128]{0,1:T(8,128)(2,1)}), bf16[16384,128]{0,1:T(8,128)(2,1)}) %all-gather.6.cloned.1.call-update) | async-done | bytes 4194320 | tf_op jit(solution)/shard_map/all_gather | solution.py:128
  168.8 4.3 %fusion.56 = f32[128,512]{1,0:T(8,128)S(1)} fusion(f32[512,2048]{0,1:T(8,128)} %bitcast_select_fusion.7, bf16[512,128]{1,0:T(8,128)(2,1)S(1)} %copy-done.11, f32[2048]{0:T(1024)S(1)} %bitcast.533, bf16[3,16384,1,128]{3,1,2,0:T(8,128)(2,1)} %all-gather.4.cloned.1.call-done, bf16[16384,128]{0,1:T(8,128)(2,1)} %all-gather.6.cloned.1.call-done), kind=kOutput, calls=%fused_computation.98 | convolution fusion | flops 541065216 | bytes 5644288 | tf_op jit(solution)/shard_map/hcr,rhd->chd/dot_general | solution.py:67
  173.2 3.9 %fusion.71 = f32[128,512]{1,0:T(8,128)S(1)} fusion(f32[128,512]{1,0:T(8,128)S(1)} %fusion.56, f32[512,2048]{0,1:T(8,128)} %bitcast_select_fusion.6, bf16[512,128]{1,0:T(8,128)(2,1)S(1)} %copy-done.11, f32[2048]{0:T(1024)S(1)} %bitcast.532, bf16[3,16384,1,128]{3,1,2,0:T(8,128)(2,1)} %all-gather.4.cloned.1.call-done, ...), kind=kOutput, calls=%fused_computation.113 | convolution fusion | flops 541130752 | bytes 5906432 | tf_op jit(solution)/shard_map/hcr,rhd->chd/dot_general | solution.py:67
  177.1 3.9 %fusion.70 = f32[128,512]{1,0:T(8,128)S(1)} fusion(f32[128,512]{1,0:T(8,128)S(1)} %fusion.71, f32[512,2048]{0,1:T(8,128)} %bitcast_select_fusion.5, bf16[512,128]{1,0:T(8,128)(2,1)S(1)} %copy-done.11, f32[2048]{0:T(1024)S(1)} %bitcast.531, bf16[3,16384,1,128]{3,1,2,0:T(8,128)(2,1)} %all-gather.4.cloned.1.call-done, ...), kind=kOutput, calls=%fused_computation.112 | convolution fusion | flops 541130752 | bytes 5906432 | tf_op jit(solution)/shard_map/hcr,rhd->chd/dot_general | solution.py:67
  180.9 3.9 %fusion.69 = f32[128,512]{1,0:T(8,128)S(1)} fusion(f32[128,512]{1,0:T(8,128)S(1)} %fusion.70, f32[512,2048]{0,1:T(8,128)} %bitcast_select_fusion.4, bf16[512,128]{1,0:T(8,128)(2,1)S(1)} %copy-done.11, f32[2048]{0:T(1024)S(1)} %bitcast.530, bf16[3,16384,1,128]{3,1,2,0:T(8,128)(2,1)} %all-gather.4.cloned.1.call-done, ...), kind=kOutput, calls=%fused_computation.111 | convolution fusion | flops 541130752 | bytes 5906432 | tf_op jit(solution)/shard_map/hcr,rhd->chd/dot_general | solution.py:67
  184.8 3.9 %fusion.68 = f32[128,512]{1,0:T(8,128)S(1)} fusion(f32[128,512]{1,0:T(8,128)S(1)} %fusion.69, f32[512,2048]{0,1:T(8,128)} %bitcast_select_fusion.3, bf16[512,128]{1,0:T(8,128)(2,1)S(1)} %copy-done.11, f32[2048]{0:T(1024)S(1)} %bitcast.529, bf16[3,16384,1,128]{3,1,2,0:T(8,128)(2,1)} %all-gather.4.cloned.1.call-done, ...), kind=kOutput, calls=%fused_computation.110 | convolution fusion | flops 541130752 | bytes 5906432 | tf_op jit(solution)/shard_map/hcr,rhd->chd/dot_general | solution.py:67
  188.7 3.9 %fusion.67 = f32[128,512]{1,0:T(8,128)S(1)} fusion(f32[128,512]{1,0:T(8,128)S(1)} %fusion.68, f32[512,2048]{0,1:T(8,128)} %bitcast_select_fusion.2, bf16[512,128]{1,0:T(8,128)(2,1)S(1)} %copy-done.11, f32[2048]{0:T(1024)S(1)} %bitcast.528, bf16[3,16384,1,128]{3,1,2,0:T(8,128)(2,1)} %all-gather.4.cloned.1.call-done, ...), kind=kOutput, calls=%fused_computation.109 | convolution fusion | flops 541130752 | bytes 5906432 | tf_op jit(solution)/shard_map/hcr,rhd->chd/dot_general | solution.py:67
  192.6 3.9 %fusion.66 = f32[128,512]{1,0:T(8,128)S(1)} fusion(f32[128,512]{1,0:T(8,128)S(1)} %fusion.67, f32[512,2048]{0,1:T(8,128)} %bitcast_select_fusion.1, bf16[512,128]{1,0:T(8,128)(2,1)S(1)} %copy-done.11, f32[2048]{0:T(1024)S(1)} %bitcast.527, bf16[3,16384,1,128]{3,1,2,0:T(8,128)(2,1)} %all-gather.4.cloned.1.call-done, ...), kind=kOutput, calls=%fused_computation.108 | convolution fusion | flops 541130752 | bytes 5906432 | tf_op jit(solution)/shard_map/hcr,rhd->chd/dot_general | solution.py:67
  196.4 4.4 %bitcast_select_fusion = f32[512,2048]{0,1:T(8,128)} fusion(bf16[512,128]{1,0:T(8,128)(2,1)S(1)} %copy-done.10, f32[2048]{0:T(1024)S(1)} %bitcast.526, s32[512]{0:T(512)S(1)} %dynamic_slice.27, s32[2048]{0:T(1024)S(1)} %get-tuple-element.29, pred[512,16]{0,1:T(8,128)(4,1)S(1)} %bitcast.550, bf16[3,16384,1,128]{3,1,2,0:T(8,128)(2,1)} %all-gather.4.cloned.1.call-done), kind=kOutput, calls=%fused_computation.20 | convolution fusion | flops 273678336 | bytes 4876288 | tf_op jit(solution)/shard_map/chd,rhd->hcr/dot_general | solution.py:56
  200.9 3.9 %fusion.103 = bf16[512,128]{0,1:T(8,128)(2,1)S(1)} fusion(f32[128,512]{1,0:T(8,128)S(1)} %fusion.66, f32[512,2048]{0,1:T(8,128)} %bitcast_select_fusion, bf16[512,128]{1,0:T(8,128)(2,1)S(1)} %copy-done.11, f32[2048]{0:T(1024)S(1)} %bitcast.525, bf16[3,16384,1,128]{3,1,2,0:T(8,128)(2,1)} %all-gather.4.cloned.1.call-done, ...), kind=kOutput, calls=%fused_computation.135 | convolution fusion | flops 541196288 | bytes 5775360 | tf_op jit(solution)/shard_map/hcr,rhd->chd/dot_general | solution.py:67
  206.6 3.0 fusion.50
  217.8 4.0 %fusion.108 = f32[2048,512]{1,0:T(8,128)} fusion(bf16[512,128]{1,0:T(8,128)(2,1)S(1)} %copy-done.12, bf16[3,16384,1,128]{3,1,2,0:T(8,128)(2,1)} %all-gather.4.cloned.1.call-done), kind=kOutput, calls=%fused_computation.163 | convolution fusion | flops 268435456 | bytes 4849664 | tf_op jit(solution)/shard_map/rhd,chd->hrc/dot_general | solution.py:42
  221.8 3.7 %fusion.109 = f32[2048,512]{1,0:T(8,128)} fusion(bf16[512,128]{1,0:T(8,128)(2,1)S(1)} %copy-done.12, bf16[3,16384,1,128]{3,1,2,0:T(8,128)(2,1)} %all-gather.4.cloned.1.call-done), kind=kOutput, calls=%fused_computation.164 | convolution fusion | flops 268435456 | bytes 4849664 | tf_op jit(solution)/shard_map/rhd,chd->hrc/dot_general | solution.py:42
  229.1 3.2 %fusion.39 = bf16[512,2048]{0,1:T(8,128)(2,1)} fusion(f32[2048,512]{1,0:T(8,128)S(1)} %fusion.107, bf16[512,128]{0,1:T(8,128)(2,1)S(1)} %copy-done.9, f32[512]{0:T(512)S(1)} %get-tuple-element.45, f32[512]{0:T(512)S(1)} %bitcast.517, s32[512]{0:T(512)S(1)} %dynamic_slice.27, s32[2048]{0:T(1024)S(1)} %get-tuple-element.35, ...), kind=kOutput, calls=%fused_computation.80 | convolution fusion | flops 277872640 | bytes 6969344 | tf_op jit(solution)/shard_map/rhd,chd->hrc/dot_general | solution.py:46
  240.2 3.7 %fusion.36 = bf16[512,2048]{0,1:T(8,128)(2,1)S(1)} fusion(f32[2048,512]{1,0:T(8,128)} %fusion.108, bf16[512,128]{0,1:T(8,128)(2,1)S(1)} %copy-done.9, f32[512]{0:T(512)S(1)} %get-tuple-element.45, f32[512]{0:T(512)S(1)} %bitcast.518, s32[512]{0:T(512)S(1)} %dynamic_slice.27, s32[2048]{0:T(1024)S(1)} %get-tuple-element.34, ...), kind=kOutput, calls=%fused_computation.76 | convolution fusion | flops 277872640 | bytes 6969344 | tf_op jit(solution)/shard_map/rhd,chd->hrc/dot_general | solution.py:46
  256.9 3.0 fusion.18
  259.9 4.2 %fusion.102 = f32[512,1024]{1,0:T(8,128)} fusion(bf16[1024,128]{1,0:T(8,128)(2,1)S(1)} %copy-done.15, f32[128,512]{1,0:T(8,128)S(1)} %convolution_add_fusion.1, bf16[512,2048]{0,1:T(8,128)(2,1)} %fusion.18, bf16[3,16384,1,128]{3,1,2,0:T(8,128)(2,1)} %all-gather.4.cloned.1.call-done), kind=kOutput, calls=%fused_computation.134 | convolution fusion | flops 402784256 | bytes 5242880 | tf_op jit(solution)/shard_map/dot_general | solution.py:169
  264.1 4.1 %fusion.64 = bf16[64,8,8,128]{3,2,1,0:T(8,128)(2,1)S(1)} fusion(bf16[1024,128]{1,0:T(8,128)(2,1)} %param.24, f32[512,1024]{1,0:T(8,128)} %fusion.102, f32[512,1024]{1,0:T(8,128)S(1)} %copy-done.13, f32[128,512]{1,0:T(8,128)} %fusion.87, f32[512,2048]{0,1:T(8,128)} %bitcast_select_fusion, bf16[16384,128]{0,1:T(8,128)(2,1)} %all-gather.6.cloned.1.call-done), kind=kOutput, calls=%fused_computation.106 | convolution fusion | flops 405405696 | bytes 10485760 | tf_op jit(solution)/shard_map/dot_general | solution.py:171
  268.4 38.8 %all_to_all.5 = bf16[8,128,512]{1,2,0:T(8,128)(2,1)S(1)} all-to-all(bf16[8,128,512]{1,2,0:T(8,128)(2,1)S(1)} %bitcast.513), channel_id=1, replica_groups=mesh['seq'=32,'head'=8] {'head'}, dimensions={0} | all-to-all | bytes 2097152 | tf_op jit(solution)/shard_map/all_to_all | solution.py:174
  (164 shorter events, 54.3 us)
Async XLA Ops:
  6.5 198.2 %copy-start = (bf16[1024,128]{1,0:T(8,128)(2,1)S(1)}, bf16[1024,128]{1,0:T(8,128)(2,1)}, u32[]{:S(2)}) copy-start(bf16[1024,128]{1,0:T(8,128)(2,1)} %param.23) | copy-start | bytes 786436
  6.5 25.5 %copy-start.17 = (bf16[512,128]{1,0:T(8,128)(2,1)S(1)}, bf16[512,128]{1,0:T(8,128)(2,1)}, u32[]{:S(2)}) copy-start(bf16[512,128]{1,0:T(8,128)(2,1)} %param.17) | copy-start | bytes 393220
  6.5 44.4 %copy-start.20 = (s32[4]{0:T(128)S(1)}, s32[4]{0:T(128)}, u32[]{:S(2)}) copy-start(s32[4]{0:T(128)} %param.21) | copy-start | bytes 52
  6.5 44.5 %copy-start.19 = (s32[4,48]{1,0:T(4,128)S(1)}, s32[4,48]{1,0:T(4,128)}, u32[]{:S(2)}) copy-start(s32[4,48]{1,0:T(4,128)} %param.20) | copy-start | bytes 2308
  6.5 46.4 %copy-start.18 = (s32[16384]{0:T(1024)S(1)}, s32[16384]{0:T(1024)}, u32[]{:S(2)}) copy-start(s32[16384]{0:T(1024)} %param.19) | copy-start | bytes 196612
  6.5 46.5 %copy-start.16 = (f32[1,512]{1,0:T(1,128)S(1)}, f32[1,512]{1,0:T(1,128)}, u32[]{:S(2)}) copy-start(f32[1,512]{1,0:T(1,128)} %param.18) | copy-start | bytes 6148
  6.6 98.6 %all-gather.4.cloned.1.call-start = ((), (), s32[]{:S(2)}) async-start(), calls=%async_computation.1 | async-start | bytes 12976128 | tf_op jit(solution)/shard_map/all_gather | solution.py:125
  8.6 96.6 %copy-start.10 = (bf16[512,128]{1,0:T(8,128)(2,1)S(1)}, bf16[512,128]{1,0:T(8,128)(2,1)}, u32[]{:S(2)}) copy-start(bf16[512,128]{1,0:T(8,128)(2,1)} %param.14) | copy-start | bytes 393220
  8.6 160.2 %all-gather.6.cloned.1.call-start = ((), (), s32[]{:S(2)}) async-start(), calls=%async_computation.2 | async-start | bytes 4325376 | tf_op jit(solution)/shard_map/all_gather | solution.py:128
  8.6 23.3 %collective-permute-start = (bf16[512,128]{1,0:T(8,128)(2,1)}, bf16[512,128]{1,0:T(8,128)(2,1)S(1)}, u32[]{:S(2)}, u32[]{:S(2)}) collective-permute-start(bf16[512,128]{1,0:T(8,128)(2,1)} %param.17), channel_id=1, source_target_pairs={{0,1},{1,2},{2,3},{3,4},{4,5},{5,6},{6,7},{7,0},{8,9},{9,10},{10,1... | collective-permute-start | bytes 393224 | tf_op jit(solution)/shard_map/ppermute | solution.py:13
  15.0 18.5 %collective-permute-start.1 = (bf16[512,128]{1,0:T(8,128)(2,1)}, bf16[512,128]{1,0:T(8,128)(2,1)S(1)}, u32[]{:S(2)}, u32[]{:S(2)}) collective-permute-start(bf16[512,128]{1,0:T(8,128)(2,1)} %param.17), channel_id=1, source_target_pairs={{0,2},{1,3},{2,4},{3,5},{4,6},{5,7},{6,0},{7,1},{8,10},{9,11},{10,... | collective-permute-start | bytes 393224 | tf_op jit(solution)/shard_map/ppermute | solution.py:13
  16.5 18.7 %collective-permute-start.2 = (bf16[512,128]{1,0:T(8,128)(2,1)}, bf16[512,128]{1,0:T(8,128)(2,1)S(1)}, u32[]{:S(2)}, u32[]{:S(2)}) collective-permute-start(bf16[512,128]{1,0:T(8,128)(2,1)} %param.17), channel_id=1, source_target_pairs={{0,3},{1,4},{2,5},{3,6},{4,7},{5,0},{6,1},{7,2},{8,11},{9,12},{10,... | collective-permute-start | bytes 393224 | tf_op jit(solution)/shard_map/ppermute | solution.py:13
  17.7 17.6 %collective-permute-start.3 = (bf16[512,128]{1,0:T(8,128)(2,1)}, bf16[512,128]{1,0:T(8,128)(2,1)S(1)}, u32[]{:S(2)}, u32[]{:S(2)}) collective-permute-start(bf16[512,128]{1,0:T(8,128)(2,1)} %param.17), channel_id=1, source_target_pairs={{0,4},{1,5},{2,6},{3,7},{4,0},{5,1},{6,2},{7,3},{8,12},{9,13},{10,... | collective-permute-start | bytes 393224 | tf_op jit(solution)/shard_map/ppermute | solution.py:13
  19.7 21.8 %collective-permute-start.4 = (bf16[512,128]{1,0:T(8,128)(2,1)}, bf16[512,128]{1,0:T(8,128)(2,1)S(1)}, u32[]{:S(2)}, u32[]{:S(2)}) collective-permute-start(bf16[512,128]{1,0:T(8,128)(2,1)} %param.17), channel_id=1, source_target_pairs={{0,5},{1,6},{2,7},{3,0},{4,1},{5,2},{6,3},{7,4},{8,13},{9,14},{10,... | collective-permute-start | bytes 393224 | tf_op jit(solution)/shard_map/ppermute | solution.py:13
  32.0 9.6 %collective-permute-start.5 = (bf16[512,128]{1,0:T(8,128)(2,1)S(1)}, bf16[512,128]{1,0:T(8,128)(2,1)S(1)}, u32[]{:S(2)}, u32[]{:S(2)}) collective-permute-start(bf16[512,128]{1,0:T(8,128)(2,1)S(1)} %copy-done.17), channel_id=1, source_target_pairs={{0,6},{1,7},{2,0},{3,1},{4,2},{5,3},{6,4},{7,5},{8,14},{9,15},{10,... | collective-permute-start | bytes 393224 | tf_op jit(solution)/shard_map/ppermute | solution.py:13
  33.6 16.2 %collective-permute-start.6 = (bf16[512,128]{1,0:T(8,128)(2,1)S(1)}, bf16[512,128]{1,0:T(8,128)(2,1)S(1)}, u32[]{:S(2)}, u32[]{:S(2)}) collective-permute-start(bf16[512,128]{1,0:T(8,128)(2,1)S(1)} %copy-done.17), channel_id=1, source_target_pairs={{0,7},{1,0},{2,1},{3,2},{4,3},{5,4},{6,5},{7,6},{8,15},{9,8},{10,9... | collective-permute-start | bytes 393224 | tf_op jit(solution)/shard_map/ppermute | solution.py:13
  127.5 41.3 %copy-start.11 = (bf16[512,128]{1,0:T(8,128)(2,1)S(1)}, bf16[512,128]{1,0:T(8,128)(2,1)}, u32[]{:S(2)}) copy-start(bf16[512,128]{1,0:T(8,128)(2,1)} %param.15) | copy-start | bytes 393220
  204.8 4.8 %copy-start.5 = (f32[512,2048]{0,1:T(8,128)S(1)}, f32[512,2048]{0,1:T(8,128)}, u32[]{:S(2)}) copy-start(f32[512,2048]{0,1:T(8,128)} %bitcast_select_fusion.6) | copy-start | bytes 12582916
  206.6 5.5 %copy-start.6 = (f32[512,2048]{0,1:T(8,128)S(1)}, f32[512,2048]{0,1:T(8,128)}, u32[]{:S(2)}) copy-start(f32[512,2048]{0,1:T(8,128)} %bitcast_select_fusion.3) | copy-start | bytes 12582916
  209.6 4.8 %copy-start.7 = (f32[512,2048]{0,1:T(8,128)S(1)}, f32[512,2048]{0,1:T(8,128)}, u32[]{:S(2)}) copy-start(f32[512,2048]{0,1:T(8,128)} %bitcast_select_fusion.1) | copy-start | bytes 12582916
  212.0 4.1 %copy-start.12 = (bf16[512,128]{1,0:T(8,128)(2,1)S(1)}, bf16[512,128]{1,0:T(8,128)(2,1)}, u32[]{:S(2)}) copy-start(bf16[512,128]{1,0:T(8,128)(2,1)} %param.13) | copy-start | bytes 393220
  212.0 13.5 %slice-start = ((s8[12582912]{0:T(1024)(128)(4,1)}), s8[4194304]{0:T(1024)(128)(4,1)S(1)}, s32[]{:S(2)}) async-start(s8[12582912]{0:T(1024)(128)(4,1)} %bitcast.508), calls=%async_computation.3 | async-start | bytes 8388608
  214.4 11.1 %slice-start.1 = ((s8[12582912]{0:T(1024)(128)(4,1)}), s8[4194304]{0:T(1024)(128)(4,1)S(1)}, s32[]{:S(2)}) async-start(s8[12582912]{0:T(1024)(128)(4,1)} %bitcast.508), calls=%async_computation.4 | async-start | bytes 8388608
  217.8 7.7 %slice-start.2 = ((s8[12582912]{0:T(1024)(128)(4,1)}), s8[4194304]{0:T(1024)(128)(4,1)S(1)}, s32[]{:S(2)}) async-start(s8[12582912]{0:T(1024)(128)(4,1)} %bitcast.508), calls=%async_computation.5 | async-start | bytes 8388608
  229.1 5.4 %copy-start.2 = (f32[512,2048]{0,1:T(8,128)S(1)}, f32[512,2048]{0,1:T(8,128)}, u32[]{:S(2)}) copy-start(f32[512,2048]{0,1:T(8,128)} %bitcast_select_fusion.7) | copy-start | bytes 12582916
  232.3 4.0 %copy-start.3 = (f32[512,2048]{0,1:T(8,128)S(1)}, f32[512,2048]{0,1:T(8,128)}, u32[]{:S(2)}) copy-start(f32[512,2048]{0,1:T(8,128)} %bitcast_select_fusion.4) | copy-start | bytes 12582916
  232.3 4.0 %copy-start.14 = (f32[128,512]{1,0:T(8,128)S(1)}, f32[128,512]{1,0:T(8,128)}, u32[]{:S(2)}) copy-start(f32[128,512]{1,0:T(8,128)} %fusion.46) | copy-start | bytes 786436
  234.6 3.3 %copy-start.4 = (f32[512,2048]{0,1:T(8,128)S(1)}, f32[512,2048]{0,1:T(8,128)}, u32[]{:S(2)}) copy-start(f32[512,2048]{0,1:T(8,128)} %bitcast_select_fusion.2) | copy-start | bytes 12582916
  240.2 4.2 %copy-start.8 = (f32[2048,512]{1,0:T(8,128)S(1)}, f32[2048,512]{1,0:T(8,128)}, u32[]{:S(2)}) copy-start(f32[2048,512]{1,0:T(8,128)} %fusion.109) | copy-start | bytes 12582916
  256.9 3.0 copy-start.15
  259.9 4.2 %copy-start.13 = (f32[512,1024]{1,0:T(8,128)S(1)}, f32[512,1024]{1,0:T(8,128)}, u32[]{:S(2)}) copy-start(f32[512,1024]{1,0:T(8,128)} %fusion.156) | copy-start | bytes 6291460
  264.1 43.9 %copy-start.1 = (bf16[1024,128]{1,0:T(8,128)(2,1)S(1)}, bf16[1024,128]{1,0:T(8,128)(2,1)}, u32[]{:S(2)}) copy-start(bf16[1024,128]{1,0:T(8,128)(2,1)} %param.23) | copy-start | bytes 786436
  (1 other events, 1.4 us)
Sparse Core Ops, SparseCore 0:
  9.2 95.9 all-gather.3
  107.1 61.7 all-gather.5
